TPU v7x, 32 devices: a whole 2x2x4 slice. The times are simulated.
32 devices in a mesh: ctx: 16 (over z, y, x), head: 2 (over core).
Axes of the slice: x: 2, y: 2, z: 4, core: 2. Of those that a mesh axis runs over, the one named last changes fastest.
Arguments:
- queries: bfloat16 [2048, 4096], P('ctx', 'head'), may hold values from -48 to 48
- keys: bfloat16 [2048, 2048], P('ctx', 'head'), may hold values from -6 to 6
- values: bfloat16 [2048, 2048], P('ctx', 'head'), may hold values from -6 to 6
- hidden_in: bfloat16 [2048, 4608], P('ctx', 'head'), may hold values from -6 to 6
- out_weight: bfloat16 [4096, 4608], P('ctx', 'head'), may hold values from -0.09375 to 0.09375
- out_gain: float32 [4608], P('head'), may hold values from 0.1 to 1.9
- reward_weight: float32 [4608], P('head'), may hold values from -0.09375 to 0.09375
- doc_lengths: int32 [16], replicated, may hold values from 1 to 1024, 2048 in all
Outputs:
- hidden_out: bfloat16 [2048, 4608], P('ctx', 'head')
- rewards: float32 [16], replicated
Inputs may be any that keep to these rules, and one draw needn't show every extreme that they name: `doc_lengths`: the lengths sum to 2048; the longest is exactly 1024.
All inputs are finite; a program needn't handle non-finite values.
Results may differ from a plain program's by a relative error of at most 0.005.
Values may be sent and summed in bfloat16 or wider, within the bound.
No kernel may reach another device: no remote copies, remote signals or barrier semaphores. Data moves between devices by JAX's collectives and lax.ppermute only.
A program may use at most 128 MiB of HBM per device.

v0:
```python
import jax
import jax.numpy as jnp
from jax import lax
from jax.sharding import Mesh, PartitionSpec as P

D = 4608
QUERY_HEADS = 32
KEY_VALUE_HEADS = 16
HEAD_WIDTH = 128
NDOC = 16
soft_cap = 50.0
CTX = ("ca", "cb")


def storage_positions(rows, tok_dev, n_ctx):
    owner = rows // tok_dev
    offset = rows % tok_dev
    half = tok_dev // 2
    slab = jnp.where(offset < half, owner, 2 * n_ctx - 1 - owner)
    return slab * half + offset % half


def document_of(positions, doc_ends):
    return jnp.sum((positions[:, None] >= doc_ends[None, :]).astype(jnp.int32), axis=1)


def shards(queries, keys, values, hidden_in, out_weight, out_gain, reward_weight, doc_lengths):
    n_ctx = lax.axis_size(CTX)
    device = lax.axis_index(CTX)
    tok_dev = queries.shape[0]
    kv_local = keys.shape[1] // HEAD_WIDTH
    group_repeat = QUERY_HEADS // KEY_VALUE_HEADS
    scale = (D / QUERY_HEADS) ** (-0.5)
    doc_ends = jnp.cumsum(doc_lengths)
    local_rows = device * tok_dev + jnp.arange(tok_dev, dtype=jnp.int32)
    query_pos = storage_positions(local_rows, tok_dev, n_ctx)
    query_doc = document_of(query_pos, doc_ends)
    q_groups = queries.reshape(tok_dev, kv_local, group_repeat, HEAD_WIDTH)
    span = tok_dev * max(1, 2048 // tok_dev)

    def attend_block(state, key_piece, value_piece, start):
        count = key_piece.shape[0]
        key_rows = start + jnp.arange(count, dtype=jnp.int32)
        key_pos = storage_positions(key_rows, tok_dev, n_ctx)
        key_doc = document_of(key_pos, doc_ends)
        visible = (query_doc[:, None] == key_doc[None, :]) & (
            key_pos[None, :] <= query_pos[:, None]
        )

        def compute(carry):
            numerator, denominator = carry
            scores = (
                jnp.einsum(
                    "qgrd,kgd->grqk",
                    q_groups,
                    key_piece.reshape(count, kv_local, HEAD_WIDTH),
                    preferred_element_type=jnp.float32,
                )
                * scale
            )
            scores = soft_cap * jnp.tanh(scores / soft_cap)
            weights = jnp.where(visible[None, None], jnp.exp(scores), 0.0)
            numerator = numerator + jnp.einsum(
                "grqk,kgd->grqd",
                weights.astype(jnp.bfloat16),
                value_piece.reshape(count, kv_local, HEAD_WIDTH),
                preferred_element_type=jnp.float32,
            )
            denominator = denominator + jnp.sum(weights, axis=-1)
            return (numerator, denominator)

        return lax.cond(jnp.any(visible), compute, lambda carry: carry, state)

    def attend(state, key_piece, value_piece, start):
        count = key_piece.shape[0]
        if count <= span:
            return attend_block(state, key_piece, value_piece, start)
        blocks = count // span
        whole = blocks * span
        width = key_piece.shape[1]
        key_blocks = key_piece[:whole].reshape(blocks, span, width)
        value_blocks = value_piece[:whole].reshape(blocks, span, width)
        starts = start + span * jnp.arange(blocks, dtype=jnp.int32)

        def step_fn(carry, item):
            return (attend_block(carry, item[0], item[1], item[2]), None)

        state, _ = lax.scan(step_fn, state, (key_blocks, value_blocks, starts))
        if whole < count:
            state = attend_block(state, key_piece[whole:], value_piece[whole:], start + whole)
        return state

    initial = (
        jnp.zeros((kv_local, group_repeat, tok_dev, HEAD_WIDTH), jnp.float32),
        jnp.zeros((kv_local, group_repeat, tok_dev), jnp.float32),
    )
    kv_width = keys.shape[1]
    both = lax.all_gather(jnp.concatenate([keys, values], axis=1), CTX, axis=0, tiled=True)
    numerator, denominator = attend(initial, both[:, :kv_width], both[:, kv_width:], jnp.int32(0))
    attended = (numerator / denominator[..., None]).astype(jnp.bfloat16)
    attended = attended.transpose(2, 0, 1, 3).reshape(tok_dev, kv_local * group_repeat * HEAD_WIDTH)
    all_heads = lax.all_gather(attended, "head", axis=1, tiled=True)
    weight_rows = lax.all_gather(out_weight, "cb", axis=0, tiled=True)
    regrouped = lax.all_to_all(all_heads, "ca", 1, 0, tiled=True)
    partial = jnp.dot(regrouped, weight_rows, preferred_element_type=jnp.float32)
    mixed = lax.psum_scatter(partial, "ca", scatter_dimension=0, tiled=True)
    squares = lax.psum(jnp.sum(mixed * mixed, axis=1), "head")
    normed = mixed / jnp.sqrt(squares / D + 1e-06)[:, None]
    out32 = hidden_in.astype(jnp.float32) + normed * out_gain[None, :]
    tok_reward = jnp.sum(out32 * reward_weight[None, :], axis=1)
    onehot = (query_doc[:, None] == jnp.arange(NDOC, dtype=jnp.int32)[None, :]).astype(jnp.float32)
    partial_sums = jnp.sum(onehot * tok_reward[:, None], axis=0)
    totals = lax.psum(partial_sums, CTX + ("head",))
    rewards = totals / jnp.sqrt(doc_lengths.astype(jnp.float32))
    return (out32.astype(jnp.bfloat16), rewards)


def solution(mesh):
    n_ctx, n_head = mesh.devices.shape
    inner = 1
    while inner * inner * 4 <= n_ctx:
        inner *= 2
    split = Mesh(mesh.devices.reshape(n_ctx // inner, inner, n_head), ("ca", "cb", "head"))
    rows = P(CTX, "head")
    in_specs = (rows, rows, rows, rows, rows, P("head"), P("head"), P())
    out_specs = (rows, P())
    return jax.shard_map(
        shards, mesh=split, in_specs=in_specs, out_specs=out_specs, check_vma=False
    )
```

profile of v0, /device:TPU:0, one launch (start us, length us, event | category | flops | bytes accessed | tf_op | source)
XLA Modules:
  0.0 398.0 jit_solution(5263270378748125020)
XLA Ops:
  7.2 0.0 all-gather.4.cloned.1.call-start
  7.2 1.1 copy.28
  8.3 1.1 copy.29
  9.5 0.8 pad_maximum_fusion
  10.3 0.0 all-gather.6.cloned.1.call-start
  10.4 0.7 copy.27
  11.1 0.1 reduce
  11.3 0.1 convert_reduce_fusion.1
  11.4 0.1 convert_reduce_fusion
  11.5 1.9 fusion.24
  14.0 142.4 %all-gather.4.cloned.1.call-done = bf16[2048,2048]{0,1:T(8,128)(2,1)} async-done(((bf16[128,2048]{0,1:T(8,128)(2,1)}), bf16[2048,2048]{0,1:T(8,128)(2,1)}) %all-gather.4.cloned.1.call-update) | async-done | bytes 8388624 | tf_op jit(solution)/shard_map/all_gather | solution.py:98
  156.4 26.9 %conditional.1 = (f32[8,2,128]{2,1,0:T(2,128)S(1)}, f32[8,2,128,128]{2,3,1,0:T(8,128)S(1)}) conditional(s32[]{:T(128)} %convert_element_type.28, () %tuple.16, (pred[128,2048]{0,1:T(8,128)(4,1)S(1)}, bf16[2048,2048]{0,1:T(8,128)(2,1)}, bf16[128,2048]{1,0:T(8,128)(2,1)}) %tuple.17), branch_computations={%region_4.5_spmd, %region_5.7_spmd} | conditional | flops 2181036032 | bytes 80748616 | solution.py:72
  156.4 6.1 %fusion.25 = (bf16[2048,1024]{0,1:T(8,128)(2,1)}, bf16[2048,1024]{0,1:T(8,128)(2,1)}) fusion(bf16[2048,2048]{0,1:T(8,128)(2,1)} %get-tuple-element.11), kind=kLoop, calls=%fused_computation.55 | loop fusion | bytes 16777216 | tf_op jit(solution)/shard_map/slice | solution.py:99
  162.4 0.4 reshape.165
  162.8 11.8 %fusion = (f32[8,2,128]{2,1,0:T(2,128)S(1)}, f32[8,2048,128,2]{2,1,3,0:T(8,128)}) fusion(pred[128,2048]{0,1:T(8,128)(4,1)S(1)} %get-tuple-element.10, bf16[2048,8,128,1]{0,2,3,1:T(8,128)(2,1)} %bitcast.30, bf16[128,8,2,128]{3,2,1,0:T(2,128)(2,1)S(1)} %reshape.165), kind=kOutput, calls=%fused_computation.1 | convolution fusion | flops 1090516992 | bytes 21766144 | tf_op jit(solution)/shard_map/cond/branch_1_fun/qgrd,kgd->grqk/dot_general | solution.py:53
  174.6 8.6 %fusion.2 = f32[8,2,128,128]{2,3,1,0:T(8,128)S(1)} fusion(bf16[2048,8,128,1]{0,2,3,1:T(8,128)(2,1)S(1)} %bitcast.29, f32[8,2048,128,2]{2,1,3,0:T(8,128)} %get-tuple-element.27, pred[128,2048]{0,1:T(8,128)(4,1)S(1)} %get-tuple-element.10), kind=kOutput, calls=%fused_computation.3 | convolution fusion | flops 1090519040 | bytes 22282240 | tf_op jit(solution)/shard_map/cond | solution.py:72
  183.2 0.9 divide_convert_fusion
  184.2 0.0 all-gather.8.cloned.1.call-start
  184.2 0.7 all-gather.8.cloned.1.call-update
  184.9 6.6 %all-gather.6.cloned.1.call-done = bf16[128,4096]{0,1:T(8,128)(2,1)} async-done(((bf16[128,2048]{0,1:T(8,128)(2,1)}), bf16[128,4096]{0,1:T(8,128)(2,1)}) %all-gather.6.cloned.1.call-update) | async-done | bytes 1048592 | tf_op jit(solution)/shard_map/all_gather | solution.py:102
  191.6 2.3 copy.31
  193.9 4.9 %all-to-all-start = ((bf16[128,4,1024]{2,0,1:T(8,128)(2,1)}), bf16[128,4,1024]{2,0,1:T(8,128)(2,1)S(1)}, u32[]{:S(2)}, u32[]{:S(2)}) async-start(bf16[128,4,1024]{2,0,1:T(8,128)(2,1)} %copy.31), calls=%async_computation | async-start | bytes 2097152 | tf_op jit(solution)/shard_map/all_to_all | solution.py:104
  198.7 53.0 %all-gather.8.cloned.1.call-done = bf16[1024,2304]{1,0:T(8,128)(2,1)} async-done(((bf16[256,2304]{1,0:T(8,128)(2,1)}), bf16[1024,2304]{1,0:T(8,128)(2,1)}) %all-gather.8.cloned.1.call-update) | async-done | bytes 4718608 | tf_op jit(solution)/shard_map/all_gather | solution.py:103
  251.7 6.6 %fusion.26 = f32[512,2304]{1,0:T(8,128)} fusion(bf16[512,1024]{1,0:T(8,128)(2,1)S(1)} %bitcast.33, bf16[1024,2304]{1,0:T(8,128)(2,1)} %all-gather.8.cloned.1.call-done), kind=kOutput, calls=%fused_computation.56 | convolution fusion | flops 2415919104 | bytes 10485760 | tf_op jit(solution)/shard_map/dot_general | solution.py:105
  258.3 0.0 reduce-scatter.2.cloned.1.call-update
  258.3 85.4 %reduce-scatter.2.cloned.1.call-done = f32[128,2304]{1,0:T(8,128)} async-done(((f32[512,2304]{1,0:T(8,128)}), f32[128,2304]{1,0:T(8,128)}) %reduce-scatter.2.cloned.1.call-update) | async-done | bytes 1179664 | tf_op jit(solution)/shard_map/reduce_scatter | solution.py:106
  343.7 1.4 multiply_reduce_fusion.1
  345.2 2.5 psum.14
  347.7 2.4 multiply_reduce_fusion
  350.1 0.1 select_reduce_fusion
  350.2 40.8 %psum.15 = f32[16]{0:T(128)S(1)} all-reduce(f32[16]{0:T(128)S(1)} %select_reduce_fusion), channel_id=1, replica_groups=mesh['ca'=4,'cb'=4,'head'=2] {'ca','cb','head'}, use_global_device_ids=true, to_apply=%region_12.13 | all-reduce | flops 16 | bytes 128 | tf_op jit(solution)/shard_map/psum | solution.py:113
  391.0 0.5 rsqrt_multiply_fusion
  (20 shorter events, 0.1 us)
Async XLA Ops:
  7.2 149.2 %all-gather.4.cloned.1.call-start = ((), (), s32[]{:S(2)}) async-start(), calls=%async_computation.2 | async-start | bytes 8912896 | tf_op jit(solution)/shard_map/all_gather | solution.py:98
  10.3 181.3 %all-gather.6.cloned.1.call-start = ((), (), s32[]{:S(2)}) async-start(), calls=%async_computation.3 | async-start | bytes 1572864 | tf_op jit(solution)/shard_map/all_gather | solution.py:102
  156.4 6.1 %copy-start.2 = (bf16[128,2048]{1,0:T(8,128)(2,1)S(1)}, bf16[128,2048]{1,0:T(8,128)(2,1)}, u32[]{:S(2)}) copy-start(bf16[128,2048]{1,0:T(8,128)(2,1)} %get-tuple-element.20) | copy-start | bytes 1572868 | tf_op jit(solution)/shard_map/cond
  162.8 11.8 %copy-start = (bf16[2048,1024]{0,1:T(8,128)(2,1)S(1)}, bf16[2048,1024]{0,1:T(8,128)(2,1)}, u32[]{:S(2)}) copy-start(bf16[2048,1024]{0,1:T(8,128)(2,1)} %get-tuple-element.24) | copy-start | bytes 12582916 | tf_op jit(solution)/shard_map/cond
  184.2 67.5 %all-gather.8.cloned.1.call-start = ((), (), s32[]{:S(2)}) async-start(), calls=%async_computation.4 | async-start | bytes 5898240 | tf_op jit(solution)/shard_map/all_gather | solution.py:103
  193.9 57.8 %all-to-all-start = ((bf16[128,4,1024]{2,0,1:T(8,128)(2,1)}), bf16[128,4,1024]{2,0,1:T(8,128)(2,1)S(1)}, u32[]{:S(2)}, u32[]{:S(2)}) async-start(bf16[128,4,1024]{2,0,1:T(8,128)(2,1)} %copy.31), calls=%async_computation | async-start | bytes 2097152 | tf_op jit(solution)/shard_map/all_to_all | solution.py:104
  198.7 145.0 %reduce-scatter.2.cloned.1.call-start = ((), (), s32[]{:S(2)}) async-start(), calls=%async_computation.5 | async-start | bytes 5898240 | tf_op jit(solution)/shard_map/reduce_scatter | solution.py:106
  258.3 89.3 %copy-start.1 = (bf16[128,2304]{1,0:T(8,128)(2,1)S(1)}, bf16[128,2304]{1,0:T(8,128)(2,1)}, u32[]{:S(2)}) copy-start(bf16[128,2304]{1,0:T(8,128)(2,1)} %param.13) | copy-start | bytes 1769476
  258.3 89.4 %copy-start.3 = (f32[2304]{0:T(1024)S(1)}, f32[2304]{0:T(1024)}, u32[]{:S(2)}) copy-start(f32[2304]{0:T(1024)} %param.16) | copy-start | bytes 27652
  258.3 89.4 %copy-start.4 = (f32[2304]{0:T(1024)S(1)}, f32[2304]{0:T(1024)}, u32[]{:S(2)}) copy-start(f32[2304]{0:T(1024)} %param.15) | copy-start | bytes 27652
  258.3 132.7 %copy-start.5 = (s32[16]{0:T(128)S(1)}, s32[16]{0:T(128)}, u32[]{:S(2)}) copy-start(s32[16]{0:T(128)} %param.17) | copy-start | bytes 196
Sparse Core Ops, SparseCore 0:
  11.3 145.0 all-gather.3
  184.3 7.2 all-gather.5
  193.4 58.2 all-gather.7
  258.5 85.2 reduce-scatter.1
where the time goes:
time: 399 us; the launch traced here: 398 us
  waiting for transfers between devices  288 us (72%)
  blocking collectives  43.2 us (11%)
  matrix products  27 us (7%)
  between operations  14.5 us (4%)
  local copies, waits for them, and re-layouts  11.7 us (3%)
  other arithmetic  8.5 us (2%)
  starting transfers between devices  4.98 us (1%)
    all_gather x1, waiting for transfers between devices, shards(): lax.all_gather(jnp.concatenate([keys, values], axis=1), CTX, axis=0, tile...  142 us
    reduce_scatter x1, waiting for transfers between devices, shards(): mixed = lax.psum_scatter(partial, 'ca', scatter_dimension=0, tiled=True)  85.4 us
    all_gather x1, waiting for transfers between devices, shards(): weight_rows = lax.all_gather(out_weight, 'cb', axis=0, tiled=True)  53 us
    psum x1, blocking collectives, shards(): totals = lax.psum(partial_sums, CTX + ('head',))  40.8 us
    dot_general x1, matrix products, compute(): jnp.einsum('qgrd,kgd->grqk', q_groups, key_piece.reshape(count, kv_local,...  11.8 us
    cond x1, matrix products, attend_block(): return lax.cond(jnp.any(visible), compute, lambda carry: carry, state)  8.62 us
  transfers between devices with their start and end apart: 5, of which 4 were waited for; matrix products, arithmetic and copies ran while one was open for 1% of the time, Pallas kernels for 0%

commit v1 on v0

--- a/solution.py
+++ b/solution.py
@@ -110,7 +110,9 @@
     tok_reward = jnp.sum(out32 * reward_weight[None, :], axis=1)
     onehot = (query_doc[:, None] == jnp.arange(NDOC, dtype=jnp.int32)[None, :]).astype(jnp.float32)
     partial_sums = jnp.sum(onehot * tok_reward[:, None], axis=0)
-    totals = lax.psum(partial_sums, CTX + ("head",))
+    mesh_axis = CTX + ("head",)
+    shards_2 = lax.all_gather(partial_sums, mesh_axis)
+    totals = jnp.sum(shards_2, axis=0)
     rewards = totals / jnp.sqrt(doc_lengths.astype(jnp.float32))
     return (out32.astype(jnp.bfloat16), rewards)
 

time: 399 us -> 399 us (level)
    psum x1 -> x0, blocking collectives: 40.8 us -> none  [shards(): totals = lax.psum(partial_sums, CTX + ('head',))]
    unnamed x0 -> x1, blocking collectives: none -> 40.7 us
where the time goes in v1:
time: 399 us; the launch traced here: 398 us
  waiting for transfers between devices  288 us (72%)
  blocking collectives  43.2 us (11%)
  matrix products  27 us (7%)
  between operations  14.5 us (4%)
  local copies, waits for them, and re-layouts  12 us (3%)
  other arithmetic  8.53 us (2%)
  starting transfers between devices  4.98 us (1%)
    all_gather x1, waiting for transfers between devices, shards(): lax.all_gather(jnp.concatenate([keys, values], axis=1), CTX, axis=0, tile...  142 us
    reduce_scatter x1, waiting for transfers between devices, shards(): mixed = lax.psum_scatter(partial, 'ca', scatter_dimension=0, tiled=True)  85.4 us
    all_gather x1, waiting for transfers between devices, shards(): weight_rows = lax.all_gather(out_weight, 'cb', axis=0, tiled=True)  53 us
    unnamed x1, blocking collectives  40.7 us
    dot_general x1, matrix products, compute(): jnp.einsum('qgrd,kgd->grqk', q_groups, key_piece.reshape(count, kv_local,...  11.8 us
    cond x1, matrix products, attend_block(): return lax.cond(jnp.any(visible), compute, lambda carry: carry, state)  8.61 us
  transfers between devices with their start and end apart: 5, of which 4 were waited for; matrix products, arithmetic and copies ran while one was open for 1% of the time, Pallas kernels for 0%

profile of v1, /device:TPU:0, one launch (start us, length us, event | category | flops | bytes accessed | tf_op | source)
XLA Modules:
  0.0 398.4 jit_solution(5564755888755323602)
XLA Ops:
  7.2 1.1 copy.28
  8.3 1.1 copy.29
  9.5 0.8 pad_maximum_fusion
  10.3 0.0 all-gather.7.cloned.1.call-start
  10.4 0.7 copy.27
  11.1 0.1 reduce
  11.3 0.1 convert_reduce_fusion.1
  11.4 0.1 convert_reduce_fusion
  11.5 1.9 fusion.24
  14.0 142.3 %all-gather.5.cloned.1.call-done = bf16[2048,2048]{0,1:T(8,128)(2,1)} async-done(((bf16[128,2048]{0,1:T(8,128)(2,1)}), bf16[2048,2048]{0,1:T(8,128)(2,1)}) %all-gather.5.cloned.1.call-update) | async-done | bytes 8388624 | tf_op jit(solution)/shard_map/all_gather | solution.py:98
  156.4 26.9 %conditional.1 = (f32[8,2,128]{2,1,0:T(2,128)S(1)}, f32[8,2,128,128]{2,3,1,0:T(8,128)S(1)}) conditional(s32[]{:T(128)} %convert_element_type.28, () %tuple.16, (pred[128,2048]{0,1:T(8,128)(4,1)S(1)}, bf16[2048,2048]{0,1:T(8,128)(2,1)}, bf16[128,2048]{1,0:T(8,128)(2,1)}) %tuple.17), branch_computations={%region_4.5_spmd, %region_5.7_spmd} | conditional | flops 2181036032 | bytes 80748616 | solution.py:72
  156.4 6.1 %fusion.25 = (bf16[2048,1024]{0,1:T(8,128)(2,1)}, bf16[2048,1024]{0,1:T(8,128)(2,1)}) fusion(bf16[2048,2048]{0,1:T(8,128)(2,1)} %get-tuple-element.11), kind=kLoop, calls=%fused_computation.55 | loop fusion | bytes 16777216 | tf_op jit(solution)/shard_map/slice | solution.py:99
  162.4 0.4 reshape.165
  162.8 11.8 %fusion = (f32[8,2,128]{2,1,0:T(2,128)S(1)}, f32[8,2048,128,2]{2,1,3,0:T(8,128)}) fusion(pred[128,2048]{0,1:T(8,128)(4,1)S(1)} %get-tuple-element.10, bf16[2048,8,128,1]{0,2,3,1:T(8,128)(2,1)} %bitcast.30, bf16[128,8,2,128]{3,2,1,0:T(2,128)(2,1)S(1)} %reshape.165), kind=kOutput, calls=%fused_computation.1 | convolution fusion | flops 1090516992 | bytes 21766144 | tf_op jit(solution)/shard_map/cond/branch_1_fun/qgrd,kgd->grqk/dot_general | solution.py:53
  174.6 8.6 %fusion.2 = f32[8,2,128,128]{2,3,1,0:T(8,128)S(1)} fusion(bf16[2048,8,128,1]{0,2,3,1:T(8,128)(2,1)S(1)} %bitcast.29, f32[8,2048,128,2]{2,1,3,0:T(8,128)} %get-tuple-element.27, pred[128,2048]{0,1:T(8,128)(4,1)S(1)} %get-tuple-element.10), kind=kOutput, calls=%fused_computation.3 | convolution fusion | flops 1090519040 | bytes 22282240 | tf_op jit(solution)/shard_map/cond | solution.py:72
  183.2 0.9 divide_convert_fusion
  184.2 0.0 all-gather.9.cloned.1.call-start
  184.2 0.7 all-gather.9.cloned.1.call-update
  184.9 6.6 %all-gather.7.cloned.1.call-done = bf16[128,4096]{0,1:T(8,128)(2,1)} async-done(((bf16[128,2048]{0,1:T(8,128)(2,1)}), bf16[128,4096]{0,1:T(8,128)(2,1)}) %all-gather.7.cloned.1.call-update) | async-done | bytes 1048592 | tf_op jit(solution)/shard_map/all_gather | solution.py:102
  191.6 2.3 copy.31
  193.9 4.9 %all-to-all-start = ((bf16[128,4,1024]{2,0,1:T(8,128)(2,1)}), bf16[128,4,1024]{2,0,1:T(8,128)(2,1)S(1)}, u32[]{:S(2)}, u32[]{:S(2)}) async-start(bf16[128,4,1024]{2,0,1:T(8,128)(2,1)} %copy.31), calls=%async_computation | async-start | bytes 2097152 | tf_op jit(solution)/shard_map/all_to_all | solution.py:104
  198.7 53.0 %all-gather.9.cloned.1.call-done = bf16[1024,2304]{1,0:T(8,128)(2,1)} async-done(((bf16[256,2304]{1,0:T(8,128)(2,1)}), bf16[1024,2304]{1,0:T(8,128)(2,1)}) %all-gather.9.cloned.1.call-update) | async-done | bytes 4718608 | tf_op jit(solution)/shard_map/all_gather | solution.py:103
  251.7 6.6 %fusion.26 = f32[512,2304]{1,0:T(8,128)} fusion(bf16[512,1024]{1,0:T(8,128)(2,1)S(1)} %bitcast.33, bf16[1024,2304]{1,0:T(8,128)(2,1)} %all-gather.9.cloned.1.call-done), kind=kOutput, calls=%fused_computation.56 | convolution fusion | flops 2415919104 | bytes 10485760 | tf_op jit(solution)/shard_map/dot_general | solution.py:105
  258.3 85.4 %reduce-scatter.2.cloned.1.call-done = f32[128,2304]{1,0:T(8,128)} async-done(((f32[512,2304]{1,0:T(8,128)}), f32[128,2304]{1,0:T(8,128)}) %reduce-scatter.2.cloned.1.call-update) | async-done | bytes 1179664 | tf_op jit(solution)/shard_map/reduce_scatter | solution.py:106
  343.8 1.4 multiply_reduce_fusion.1
  345.2 2.5 psum.7
  347.7 2.4 multiply_reduce_fusion
  350.1 0.1 select_reduce_fusion
  350.2 0.2 dynamic-update-slice
  350.5 40.7 %all-reduce = f32[512]{0:T(512)S(1)} all-reduce(f32[512]{0:T(512)S(1)} %dynamic-update-slice), channel_id=2, replica_groups=mesh['ca'=4,'cb'=4,'head'=2] {'ca','cb','head'}, use_global_device_ids=true, to_apply=%add | all-reduce | flops 512 | bytes 4096
  391.2 0.1 reshape.173
  391.3 0.5 rsqrt_multiply_fusion
  (24 shorter events, 0.2 us)
Async XLA Ops:
  7.2 149.2 %all-gather.5.cloned.1.call-start = ((), (), s32[]{:S(2)}) async-start(), calls=%async_computation.2 | async-start | bytes 8912896 | tf_op jit(solution)/shard_map/all_gather | solution.py:98
  10.3 181.3 %all-gather.7.cloned.1.call-start = ((), (), s32[]{:S(2)}) async-start(), calls=%async_computation.3 | async-start | bytes 1572864 | tf_op jit(solution)/shard_map/all_gather | solution.py:102
  156.4 6.1 %copy-start.2 = (bf16[128,2048]{1,0:T(8,128)(2,1)S(1)}, bf16[128,2048]{1,0:T(8,128)(2,1)}, u32[]{:S(2)}) copy-start(bf16[128,2048]{1,0:T(8,128)(2,1)} %get-tuple-element.20) | copy-start | bytes 1572868 | tf_op jit(solution)/shard_map/cond
  162.8 11.8 %copy-start = (bf16[2048,1024]{0,1:T(8,128)(2,1)S(1)}, bf16[2048,1024]{0,1:T(8,128)(2,1)}, u32[]{:S(2)}) copy-start(bf16[2048,1024]{0,1:T(8,128)(2,1)} %get-tuple-element.24) | copy-start | bytes 12582916 | tf_op jit(solution)/shard_map/cond
  184.2 67.5 %all-gather.9.cloned.1.call-start = ((), (), s32[]{:S(2)}) async-start(), calls=%async_computation.4 | async-start | bytes 5898240 | tf_op jit(solution)/shard_map/all_gather | solution.py:103
  193.9 57.8 %all-to-all-start = ((bf16[128,4,1024]{2,0,1:T(8,128)(2,1)}), bf16[128,4,1024]{2,0,1:T(8,128)(2,1)S(1)}, u32[]{:S(2)}, u32[]{:S(2)}) async-start(bf16[128,4,1024]{2,0,1:T(8,128)(2,1)} %copy.31), calls=%async_computation | async-start | bytes 2097152 | tf_op jit(solution)/shard_map/all_to_all | solution.py:104
  198.7 145.0 %reduce-scatter.2.cloned.1.call-start = ((), (), s32[]{:S(2)}) async-start(), calls=%async_computation.5 | async-start | bytes 5898240 | tf_op jit(solution)/shard_map/reduce_scatter | solution.py:106
  258.3 89.4 %copy-start.1 = (bf16[128,2304]{1,0:T(8,128)(2,1)S(1)}, bf16[128,2304]{1,0:T(8,128)(2,1)}, u32[]{:S(2)}) copy-start(bf16[128,2304]{1,0:T(8,128)(2,1)} %param.13) | copy-start | bytes 1769476
  258.3 89.4 %copy-start.3 = (f32[2304]{0:T(1024)S(1)}, f32[2304]{0:T(1024)}, u32[]{:S(2)}) copy-start(f32[2304]{0:T(1024)} %param.16) | copy-start | bytes 27652
  258.3 89.4 %copy-start.4 = (f32[2304]{0:T(1024)S(1)}, f32[2304]{0:T(1024)}, u32[]{:S(2)}) copy-start(f32[2304]{0:T(1024)} %param.15) | copy-start | bytes 27652
  258.3 133.0 %copy-start.5 = (s32[16]{0:T(128)S(1)}, s32[16]{0:T(128)}, u32[]{:S(2)}) copy-start(s32[16]{0:T(128)} %param.17) | copy-start | bytes 196
Sparse Core Ops, SparseCore 0:
  11.3 145.0 all-gather.4
  184.3 7.2 all-gather.6
  193.4 58.2 all-gather.8
  258.4 85.2 reduce-scatter.1
